TPU v7x, 512 devices: a whole 4x4x16 slice. The times are simulated.
512 devices in a mesh: row: 16 (over x, y), col: 32 (over z, core).
Axes of the slice: x: 4, y: 4, z: 16, core: 2. Of those that a mesh axis runs over, the one named last changes fastest.
Arguments:
- hidden: bfloat16 [2560, 7168], P('col', 'row'), may hold values from -6 to 6
- ln_gain: bfloat16 [7168], P('row'), may hold values from 0.099609375 to 1.8984375
- ln_shift: bfloat16 [7168], P('row'), may hold values from -3 to 3
- qkv_weight: bfloat16 [7168, 12288], P('row', 'col'), may hold values from -0.0625 to 0.0625
- qkv_bias: bfloat16 [12288], P('col'), may hold values from -5.351432 to 5.351432
- out_weight: bfloat16 [4096, 7168], P('row', 'col'), may hold values from -0.09375 to 0.09375
- out_bias: bfloat16 [7168], P('col'), may hold values from -3 to 3
- down_qkv: bfloat16 [64, 7168, 16], P(None, 'row'), may hold values from -0.0625 to 0.0625
- up_qkv: bfloat16 [64, 16, 12288], P(None, None, 'col'), may hold values from -1.5 to 1.5
- down_out: bfloat16 [64, 16, 4096], P(None, None, 'col'), may hold values from -0.09375 to 0.09375
- up_out: bfloat16 [64, 16, 7168], P(None, None, 'col'), may hold values from -1.5 to 1.5
- prompt_lens: int32 [16], replicated, may hold values from 1 to 80, as said below
- suffix_lens: int32 [16, 16], replicated, may hold values from 1 to 5, as said below
- group_sizes: int32 [16], replicated, may hold values from 8 to 16, as said below
- group_adapter_choice: int32 [16], replicated, may hold values from 0 to 15
- chosen: int32 [16], replicated, may hold values from 0 to 63, as said below
Outputs:
- attn_out: bfloat16 [2560, 7168], P('row', 'col')
Inputs may be any that keep to these rules, and one draw needn't show every extreme that they name: `prompt_lens`: one group, drawn from the seed, has a prompt of exactly 80 tokens, 16 requests and every suffix 5 long, so it fills all 160 slots. `suffix_lens`: entries past a group's number of requests are not used. `group_sizes`: A group's prompt and its live suffixes take at most 160 slots. `chosen`: 16 different bank indices.
All inputs are finite; a program needn't handle non-finite values.
Results may differ from a plain program's by a relative error of at most 0.012.
The roundings to bfloat16 on the way count: a program that leaves them out, or rounds other values in their place, can miss the bound.
Values may be sent and summed in bfloat16 or wider, within the bound.
No kernel may reach another device: no remote copies, remote signals or barrier semaphores. Data moves between devices by JAX's collectives and lax.ppermute only.
A program may use at most 64 MiB of HBM per device.

v0:
```python
import jax
import jax.numpy as jnp
from jax import lax
from jax.sharding import PartitionSpec as P

HEAD_SIZE = 128
GCAP = 160
WIN = 53


def broadcast(x, axis, root):
    mine = lax.axis_index(axis) == root
    return lax.psum(jnp.where(mine, x, jnp.zeros_like(x)), axis)


def group_layout(prompt, count, suffix):
    offsets = jnp.arange(GCAP, dtype=jnp.int32)
    chosen_adapter_index = jnp.arange(suffix.shape[0], dtype=jnp.int32)
    live_lens = jnp.where(chosen_adapter_index < count, suffix, 0)
    end_at = prompt + jnp.cumsum(live_lens)
    group_start_rows = end_at - live_lens
    request = jnp.sum((offsets[:, None] >= end_at[None, :]).astype(jnp.int32), axis=1)
    in_prompt = offsets < prompt
    live_rows = in_prompt | (request < count)
    group_begin_row = jnp.sum(
        jnp.where(chosen_adapter_index[None, :] == request[:, None], group_start_rows[None, :], 0),
        axis=1,
    )
    position = jnp.where(in_prompt, offsets, prompt + offsets - group_begin_row)
    request_of = jnp.where(in_prompt, -1, request)
    return (live_rows, request_of, position)


def key_mask(live_rows, request_of, position):
    shared = (request_of[None, :] == -1) | (request_of[None, :] == request_of[:, None])
    causal = position[None, :] <= position[:, None]
    within = (position[:, None] - position[None, :] < WIN) | (position[None, :] == 0)
    allowed = live_rows[:, None] & live_rows[None, :] & shared & causal & within
    first_key = jnp.arange(GCAP)[None, :] == 0
    return jnp.where(live_rows[:, None], allowed, first_key)


def attention(queries, key_rows, value_rows, allowed):
    scores = jnp.einsum("qhe,khe->hqk", queries, key_rows, preferred_element_type=jnp.float32)
    scores = jnp.where(allowed[None], scores, -1e30)
    highest = jnp.max(scores, axis=2, keepdims=True)
    weights = jnp.where(allowed[None], jnp.exp(scores - highest), 0.0)
    probs = (weights / jnp.sum(weights, axis=2, keepdims=True)).astype(jnp.bfloat16)
    mixed_rows = jnp.einsum("hqk,khe->qhe", probs, value_rows, preferred_element_type=jnp.float32)
    return mixed_rows.astype(jnp.bfloat16).reshape(queries.shape[0], -1)


def local(
    hidden,
    ln_gain,
    ln_shift,
    qkv_weight,
    qkv_bias,
    out_weight,
    out_bias,
    down_qkv,
    up_qkv,
    down_out,
    up_out,
    prompt_lens,
    suffix_lens,
    group_sizes,
    group_adapter_choice,
    chosen,
):
    row_index = lax.axis_index("row")
    row_count = lax.axis_size("row")
    adapters = chosen[group_adapter_choice]
    own_adapter = adapters[row_index]
    low_rank = down_qkv.shape[2]
    features, gain_full, shift_full = (
        lax.all_gather(hidden, "row", axis=1, tiled=True),
        lax.all_gather(ln_gain, "row", axis=0, tiled=True),
        lax.all_gather(ln_shift, "row", axis=0, tiled=True),
    )
    widened = features.astype(jnp.float32)
    average = jnp.mean(widened, axis=1, keepdims=True)
    centred = widened - average
    spread = jnp.mean(centred * centred, axis=1, keepdims=True)
    normed = (
        centred * lax.rsqrt(spread + 1e-05) * gain_full.astype(jnp.float32)
        + shift_full.astype(jnp.float32)
    ).astype(jnp.bfloat16)
    per_group = lax.axis_size("col") // row_count
    received = []
    for offset in range(per_group):
        received.append(broadcast(normed, "col", row_index * per_group + offset))
    group_rows = jnp.concatenate(received, axis=0)
    lowered = jnp.transpose(down_qkv[adapters], (1, 0, 2)).reshape(
        down_qkv.shape[1], row_count * low_rank
    )
    sliced = group_rows
    own_down = lax.dynamic_slice_in_dim(
        lax.all_gather(lowered, "row", axis=0, tiled=True), row_index * low_rank, low_rank, 1
    )
    projected = jnp.dot(
        sliced,
        lax.all_gather(qkv_weight, "row", axis=0, tiled=True),
        preferred_element_type=jnp.float32,
    )
    reduced = jnp.dot(sliced, own_down, preferred_element_type=jnp.float32)
    projected = (
        projected
        + qkv_bias.astype(jnp.float32)
        + jnp.dot(
            reduced.astype(jnp.bfloat16), up_qkv[own_adapter], preferred_element_type=jnp.float32
        )
    )
    heads_here = projected.shape[1] // (3 * HEAD_SIZE)
    shaped = projected.reshape(GCAP, heads_here, 3, HEAD_SIZE)
    queries = (shaped[:, :, 0] * HEAD_SIZE ** (-0.5)).astype(jnp.bfloat16)
    key_rows = shaped[:, :, 1].astype(jnp.bfloat16)
    value_rows = shaped[:, :, 2].astype(jnp.bfloat16)
    live_rows, request_of, position = group_layout(
        prompt_lens[row_index], group_sizes[row_index], suffix_lens[row_index]
    )
    mixed_rows = attention(queries, key_rows, value_rows, key_mask(live_rows, request_of, position))
    down_here = down_out[own_adapter]
    all_heads, down_full = (
        lax.all_gather(mixed_rows, "col", axis=1, tiled=True),
        lax.all_gather(down_here, "col", axis=1, tiled=True),
    )
    reduced_out = lax.dot_general(
        all_heads, down_full, (((1,), (1,)), ((), ())), preferred_element_type=jnp.float32
    ).astype(jnp.bfloat16)
    sliced = all_heads
    combined = jnp.dot(
        sliced,
        lax.all_gather(out_weight, "row", axis=0, tiled=True),
        preferred_element_type=jnp.float32,
    )
    result = (
        combined
        + out_bias.astype(jnp.float32)
        + jnp.dot(reduced_out, up_out[own_adapter], preferred_element_type=jnp.float32)
    )
    return (result * live_rows[:, None].astype(jnp.float32)).astype(jnp.bfloat16)


def solution(mesh):
    in_specs = (
        P("col", "row"),
        P("row"),
        P("row"),
        P("row", "col"),
        P("col"),
        P("row", "col"),
        P("col"),
        P(None, "row", None),
        P(None, None, "col"),
        P(None, None, "col"),
        P(None, None, "col"),
        P(),
        P(),
        P(),
        P(),
        P(),
    )
    out_specs = P("row", "col")
    return jax.shard_map(local, mesh=mesh, in_specs=in_specs, out_specs=out_specs, check_vma=False)
```

profile of v0, /device:TPU:2, one launch (start us, length us, event | category | flops | bytes accessed | tf_op | source)
XLA Modules:
  0.0 603.2 jit_solution(5477577475409524125)
XLA Ops:
  6.5 0.0 copy-start
  6.5 0.0 all-gather.17.cloned.1.call-start
  6.5 0.7 all-gather.17.cloned.1.call-update
  7.3 0.0 all-reduce.6.cloned.1.call-start
  7.3 1.3 dynamic-slice
  9.3 0.9 dynamic-update-slice
  10.1 0.9 dynamic-update-slice.1
  11.0 69.1 %all-reduce.3 = (bf16[7168]{0:T(1024)(128)(2,1)S(1)}, bf16[7168]{0:T(1024)(128)(2,1)S(1)}) all-reduce(bf16[7168]{0:T(1024)(128)(2,1)S(1)} %dynamic-update-slice, bf16[7168]{0:T(1024)(128)(2,1)S(1)} %dynamic-update-slice.1), channel_id=1, replica_groups=mesh['row'=16,'col'=32] {'row'}, use_global_device_ids=true, to_apply=%add | all-reduce | flops 14336 | bytes 57344
  80.1 0.0 all-gather.17.cloned.1.call-done
  80.2 3.6 copy.26
  83.7 2.4 reshape.225
  86.2 1.6 convert_reduce_fusion
  87.8 0.4 multiply_reduce_fusion
  88.2 1.6 broadcast_select_fusion
  89.8 1.2 broadcast_select_fusion.1
  91.0 0.0 all-reduce.6.cloned.1.call-update
  91.0 0.0 all-gather.9.cloned.1.call-start
  91.1 0.7 all-gather.9.cloned.1.call-update
  91.7 0.0 all-gather.11.cloned.1.call-start
  91.8 0.0 copy-done.4
  91.8 0.0 copy-done.1
  91.8 0.7 gather_fusion
  92.5 0.0 copy-start.5
  92.5 0.0 copy-start.6
  92.6 0.6 gather_fusion.1
  93.1 0.8 copy.27
  94.0 0.0 all-gather.11.cloned.1.call-update
  94.0 0.0 all-gather.15.cloned.1.call-start
  94.1 0.6 dynamic_slice.25
  95.9 0.0 copy-done.5
  96.0 0.6 dynamic_slice.28
  96.6 1.3 compare_select_fusion.3
  97.9 0.1 copy.28
  98.0 0.6 dynamic_slice.27
  99.3 0.7 add_reduce_fusion
  100.1 0.1 convert_reduce_fusion.1
  100.2 1.3 fusion.54
  101.5 0.1 select_reduce_fusion
  101.6 0.6 broadcast_compare_fusion
  102.2 1.3 fusion.57
  103.5 209.5 %all-reduce.6.cloned.1.call-done = (bf16[80,7168]{1,0:T(8,128)(2,1)}, bf16[80,7168]{1,0:T(8,128)(2,1)}) async-done(((bf16[80,7168]{1,0:T(8,128)(2,1)}, bf16[80,7168]{1,0:T(8,128)(2,1)}), (bf16[80,7168]{1,0:T(8,128)(2,1)}, bf16[80,7168]{1,0:T(8,128)(2,1)})) %all-reduce.6.cloned.1.call-update) | async-done | bytes 2293776 | tf_op jit(solution)/shard_map/psum | solution.py:13
  313.0 1.4 constant_dynamic-update-slice_fusion.1
  314.4 0.2 copy-done.2
  314.6 0.1 constant_dynamic-update-slice_fusion
  314.7 74.3 %all-gather.9.cloned.1.call-done = bf16[7168,384]{1,0:T(8,128)(2,1)} async-done(((bf16[448,384]{1,0:T(8,128)(2,1)}), bf16[7168,384]{1,0:T(8,128)(2,1)}) %all-gather.9.cloned.1.call-update) | async-done | bytes 5505040 | tf_op jit(solution)/shard_map/all_gather | solution.py:103
  388.9 4.6 convolution_add_fusion.1
  393.6 62.4 %all-gather.11.cloned.1.call-done = bf16[7168,256]{1,0:T(8,128)(2,1)} async-done(((bf16[448,256]{1,0:T(8,128)(2,1)}), bf16[7168,256]{1,0:T(8,128)(2,1)}) %all-gather.11.cloned.1.call-update) | async-done | bytes 3670032 | tf_op jit(solution)/shard_map/all_gather | solution.py:99
  455.9 4.1 convolution_add_fusion
  460.0 1.1 reshape.192
  461.1 0.1 convert.4
  461.2 0.1 fusion.37
  461.3 0.2 fusion.60
  461.4 0.2 fusion.61
  461.6 0.2 fusion.36
  461.9 1.0 fusion.19
  462.9 0.0 all-gather.15.cloned.1.call-update
  462.9 0.0 all-gather.13.cloned.1.call-start
  463.0 0.5 all-gather.13.cloned.1.call-update
  463.5 0.7 constant_dynamic-slice_fusion
  464.2 31.3 %all-gather.1 = bf16[1,16,4096]{2,1,0:T(8,128)(2,1)S(1)} all-gather(bf16[1,16,128]{2,1,0:T(8,128)(2,1)S(1)} %constant_dynamic-slice_fusion), channel_id=3, replica_groups=mesh['row'=16,'col'=32] {'col'}, dimensions={2}, use_global_device_ids=true | all-gather | bytes 135168 | tf_op jit(solution)/shard_map/all_gather | solution.py:126
  495.5 37.9 %all-gather.15.cloned.1.call-done = bf16[160,1,4096]{2,0,1:T(8,128)(2,1)} async-done(((bf16[160,1,128]{2,0,1:T(8,128)(2,1)}), bf16[160,1,4096]{2,0,1:T(8,128)(2,1)}) %all-gather.15.cloned.1.call-update) | async-done | bytes 1310736 | tf_op jit(solution)/shard_map/all_gather | solution.py:125
  533.4 2.0 fusion.27
  535.5 57.6 %all-gather.13.cloned.1.call-done = bf16[4096,224]{0,1:T(8,128)(2,1)} async-done(((bf16[256,224]{0,1:T(8,128)(2,1)}), bf16[4096,224]{0,1:T(8,128)(2,1)}) %all-gather.13.cloned.1.call-update) | async-done | bytes 1835024 | tf_op jit(solution)/shard_map/all_gather | solution.py:134
  593.1 3.3 fusion.16
  (23 shorter events, 0.1 us)
Async XLA Ops:
  6.5 86.0 %copy-start = (bf16[64,448,16]{1,2,0:T(8,128)(2,1)S(1)}, bf16[64,448,16]{1,2,0:T(8,128)(2,1)}, u32[]{:S(2)}) copy-start(bf16[64,448,16]{1,2,0:T(8,128)(2,1)} %param.23) | copy-start | bytes 2752516
  6.5 73.6 %all-gather.17.cloned.1.call-start = ((), (), s32[]{:S(2)}) async-start(), calls=%async_computation.4 | async-start | bytes 1392640 | tf_op jit(solution)/shard_map/all_gather | solution.py:77
  7.3 305.7 %all-reduce.6.cloned.1.call-start = ((), (), s32[]{:S(2)}) async-start(), calls=%async_computation.5 | async-start | bytes 4587520 | tf_op jit(solution)/shard_map/psum | solution.py:13
  89.8 2.0 copy-start.4
  89.8 2.0 copy-start.1
  91.0 297.9 %all-gather.9.cloned.1.call-start = ((), (), s32[]{:S(2)}) async-start(), calls=%async_computation | async-start | bytes 5849088 | tf_op jit(solution)/shard_map/all_gather | solution.py:103
  91.7 364.2 %all-gather.11.cloned.1.call-start = ((), (), s32[]{:S(2)}) async-start(), calls=%async_computation.1 | async-start | bytes 3899392 | tf_op jit(solution)/shard_map/all_gather | solution.py:99
  92.5 1.5 copy-start.3
  92.5 3.4 copy-start.5
  92.5 5.5 copy-start.6
  94.0 439.5 %all-gather.15.cloned.1.call-start = ((), (), s32[]{:S(2)}) async-start(), calls=%async_computation.3 | async-start | bytes 1351680 | tf_op jit(solution)/shard_map/all_gather | solution.py:125
  313.0 1.6 copy-start.2
  460.0 3.4 copy-start.7
  462.9 130.2 %all-gather.13.cloned.1.call-start = ((), (), s32[]{:S(2)}) async-start(), calls=%async_computation.2 | async-start | bytes 1949696 | tf_op jit(solution)/shard_map/all_gather | solution.py:134
Sparse Core Ops, SparseCore 0:
  10.4 62.7 all-gather.16
  91.1 221.7 all-reduce.5
  316.0 72.8 all-gather.8
  391.8 64.0 all-gather.10
  463.0 70.3 all-gather.14
  536.3 56.7 all-gather.12
where the time goes:
time: 604 us; the launch traced here: 603 us
  waiting for transfers between devices  444 us (74%)
  blocking collectives  100 us (17%)
  local copies, waits for them, and re-layouts  16.6 us (3%)
  between operations  16.3 us (3%)
  matrix products  15.3 us (3%)
  other arithmetic  10.7 us (2%)
    psum x1, waiting for transfers between devices, broadcast(): return lax.psum(jnp.where(mine, x, jnp.zeros_like(x)), axis)  209 us
    all_gather x1, waiting for transfers between devices, local(): lax.all_gather(qkv_weight, 'row', axis=0, tiled=True)  74.3 us
    unnamed x1, blocking collectives  69.1 us
    all_gather x1, waiting for transfers between devices, local(): lax.all_gather(lowered, 'row', axis=0, tiled=True)  62.4 us
    all_gather x1, waiting for transfers between devices, local(): lax.all_gather(out_weight, 'row', axis=0, tiled=True)  57.6 us
    all_gather x1, waiting for transfers between devices, local(): lax.all_gather(mixed_rows, 'col', axis=1, tiled=True)  37.9 us
    all_gather x1, blocking collectives, local(): lax.all_gather(down_here, 'col', axis=1, tiled=True)  31.3 us
  transfers between devices with their start and end apart: 6, of which 5 were waited for; matrix products, arithmetic and copies ran while one was open for 4% of the time, Pallas kernels for 0%

commit v1 on v0

--- a/solution.py
+++ b/solution.py
@@ -6,6 +6,17 @@
 HEAD_SIZE = 128
 GCAP = 160
 WIN = 53
+
+
+def pass_unit_in(tile_in):
+    which_axis = "col"
+    dev_count = lax.axis_size(which_axis)
+    v_next = range(tile_in.ndim)
+    f_now = map(lambda at: dev_count if at == 1 else 1, v_next)
+    response = list(f_now)
+    parts_out = jnp.tile(tile_in, response)
+    small = lax.all_to_all(parts_out, split_axis=1, tiled=True, concat_axis=1, axis_name=which_axis)
+    return small
 
 
 def broadcast(x, axis, root):
@@ -122,7 +133,7 @@
     mixed_rows = attention(queries, key_rows, value_rows, key_mask(live_rows, request_of, position))
     down_here = down_out[own_adapter]
     all_heads, down_full = (
-        lax.all_gather(mixed_rows, "col", axis=1, tiled=True),
+        pass_unit_in(mixed_rows),
         lax.all_gather(down_here, "col", axis=1, tiled=True),
     )
     reduced_out = lax.dot_general(

time: 604 us -> 573 us (0.949)
  the two profiles are of different devices: /device:TPU:2 before, /device:TPU:1 now
where the time goes in v1:
time: 573 us; the launch traced here: 572 us
  waiting for transfers between devices  357 us (62%)
  blocking collectives  144 us (25%)
  local copies, waits for them, and re-layouts  17.8 us (3%)
  between operations  16 us (3%)
  matrix products  13.7 us (2%)
  starting transfers between devices  13.6 us (2%)
  other arithmetic  10.5 us (2%)
    psum x1, waiting for transfers between devices, broadcast(): return lax.psum(jnp.where(mine, x, jnp.zeros_like(x)), axis)  217 us
    all_gather x1, blocking collectives, local(): lax.all_gather(down_here, 'col', axis=1, tiled=True)  82.3 us
    all_gather x1, waiting for transfers between devices, local(): lax.all_gather(qkv_weight, 'row', axis=0, tiled=True)  75.2 us
    all_gather x1, waiting for transfers between devices, local(): lax.all_gather(lowered, 'row', axis=0, tiled=True)  62.6 us
    unnamed x1, blocking collectives  61.8 us
    all_to_all x1, starting transfers between devices, pass_unit_in(): lax.all_to_all(parts_out, split_axis=1, tiled=True, concat_axis=1, axis_n...  13.5 us
  transfers between devices with their start and end apart: 6, of which 3 were waited for; matrix products, arithmetic and copies ran while one was open for 4% of the time, Pallas kernels for 0%

profile of v1, /device:TPU:1, one launch (start us, length us, event | category | flops | bytes accessed | tf_op | source)
XLA Modules:
  0.0 572.4 jit_solution(7231011913092822895)
XLA Ops:
  6.5 0.7 all-gather.13.cloned.1.call-update
  7.3 0.0 all-reduce.6.cloned.1.call-start
  7.3 1.3 dynamic-slice
  9.3 0.9 dynamic-update-slice
  10.1 0.9 dynamic-update-slice.1
  11.0 61.8 %all-reduce.3 = (bf16[7168]{0:T(1024)(128)(2,1)S(1)}, bf16[7168]{0:T(1024)(128)(2,1)S(1)}) all-reduce(bf16[7168]{0:T(1024)(128)(2,1)S(1)} %dynamic-update-slice, bf16[7168]{0:T(1024)(128)(2,1)S(1)} %dynamic-update-slice.1), channel_id=1, replica_groups=mesh['row'=16,'col'=32] {'row'}, use_global_device_ids=true, to_apply=%add | all-reduce | flops 14336 | bytes 57344
  72.8 0.0 all-gather.13.cloned.1.call-done
  72.9 3.6 copy.27
  76.5 2.4 reshape.227
  78.9 1.6 convert_reduce_fusion
  80.5 0.4 multiply_reduce_fusion
  80.9 1.6 broadcast_select_fusion
  82.5 1.2 broadcast_select_fusion.1
  83.7 0.0 all-reduce.6.cloned.1.call-update
  83.7 0.0 all-gather.7.cloned.1.call-start
  83.7 0.7 all-gather.7.cloned.1.call-update
  84.4 0.0 all-gather.9.cloned.1.call-start
  84.5 0.0 copy-done.1
  84.5 0.7 gather_fusion
  85.2 0.0 copy-done
  85.2 0.0 copy-start.3
  85.2 0.0 copy-start.5
  85.2 0.0 copy-start.6
  85.2 0.6 gather_fusion.1
  85.8 0.8 copy.28
  86.6 0.0 all-gather.9.cloned.1.call-update
  86.7 0.6 dynamic_slice.25
  88.6 0.0 copy-done.5
  88.6 0.6 dynamic_slice.28
  89.2 1.3 compare_select_fusion.3
  90.4 0.1 copy.29
  90.6 0.6 dynamic_slice.27
  91.8 0.7 add_reduce_fusion
  92.6 0.1 convert_reduce_fusion.1
  92.7 1.3 fusion.56
  93.9 0.1 select_reduce_fusion
  94.0 0.6 broadcast_compare_fusion
  94.7 1.2 fusion.59
  95.9 216.8 %all-reduce.6.cloned.1.call-done = (bf16[80,7168]{1,0:T(8,128)(2,1)}, bf16[80,7168]{1,0:T(8,128)(2,1)}) async-done(((bf16[80,7168]{1,0:T(8,128)(2,1)}, bf16[80,7168]{1,0:T(8,128)(2,1)}), (bf16[80,7168]{1,0:T(8,128)(2,1)}, bf16[80,7168]{1,0:T(8,128)(2,1)})) %all-reduce.6.cloned.1.call-update) | async-done | bytes 2293776 | tf_op jit(solution)/shard_map/psum | solution.py:24
  312.7 1.4 constant_dynamic-update-slice_fusion.1
  314.1 0.2 copy-done.2
  314.3 0.1 constant_dynamic-update-slice_fusion
  314.4 75.2 %all-gather.7.cloned.1.call-done = bf16[7168,384]{1,0:T(8,128)(2,1)} async-done(((bf16[448,384]{1,0:T(8,128)(2,1)}), bf16[7168,384]{1,0:T(8,128)(2,1)}) %all-gather.7.cloned.1.call-update) | async-done | bytes 5505040 | tf_op jit(solution)/shard_map/all_gather | solution.py:114
  389.6 4.6 convolution_add_fusion.1
  394.2 62.6 %all-gather.9.cloned.1.call-done = bf16[7168,256]{1,0:T(8,128)(2,1)} async-done(((bf16[448,256]{1,0:T(8,128)(2,1)}), bf16[7168,256]{1,0:T(8,128)(2,1)}) %all-gather.9.cloned.1.call-update) | async-done | bytes 3670032 | tf_op jit(solution)/shard_map/all_gather | solution.py:110
  456.8 4.1 convolution_add_fusion
  461.0 1.0 reshape.196
  462.0 0.1 convert.4
  462.1 0.1 fusion.39
  462.2 0.2 fusion.62
  462.3 0.2 fusion.63
  462.6 0.2 fusion.38
  462.8 0.4 fusion.21
  463.2 0.0 copy-start.7
  463.2 1.2 tile.9
  464.4 13.5 %all-to-all-start = ((bf16[160,32,128]{2,0,1:T(8,128)(2,1)}), bf16[160,32,128]{2,0,1:T(8,128)(2,1)S(1)}, u32[]{:S(2)}, u32[]{:S(2)}) async-start(bf16[160,32,128]{2,0,1:T(8,128)(2,1)} %tile.9), calls=%async_computation | async-start | bytes 2621440 | tf_op jit(solution)/shard_map/all_to_all | solution.py:18
  477.9 0.0 all-gather.11.cloned.1.call-start
  478.0 0.5 all-gather.11.cloned.1.call-update
  478.5 0.7 constant_dynamic-slice_fusion
  479.2 82.3 %all-gather = bf16[1,16,4096]{2,1,0:T(8,128)(2,1)S(1)} all-gather(bf16[1,16,128]{2,1,0:T(8,128)(2,1)S(1)} %constant_dynamic-slice_fusion), channel_id=2, replica_groups=mesh['row'=16,'col'=32] {'col'}, dimensions={2}, use_global_device_ids=true | all-gather | bytes 135168 | tf_op jit(solution)/shard_map/all_gather | solution.py:137
  561.5 0.0 all-to-all-done
  561.5 1.4 fusion.29
  562.9 0.0 all-gather.11.cloned.1.call-done
  562.9 2.9 fusion.18
  (23 shorter events, 0.1 us)
Async XLA Ops:
  6.5 78.7 %copy-start = (bf16[64,448,16]{1,2,0:T(8,128)(2,1)S(1)}, bf16[64,448,16]{1,2,0:T(8,128)(2,1)}, u32[]{:S(2)}) copy-start(bf16[64,448,16]{1,2,0:T(8,128)(2,1)} %param.23) | copy-start | bytes 2752516
  6.5 66.3 %all-gather.13.cloned.1.call-start = ((), (), s32[]{:S(2)}) async-start(), calls=%async_computation.4 | async-start | bytes 1392640 | tf_op jit(solution)/shard_map/all_gather | solution.py:88
  7.3 305.5 %all-reduce.6.cloned.1.call-start = ((), (), s32[]{:S(2)}) async-start(), calls=%async_computation.5 | async-start | bytes 4587520 | tf_op jit(solution)/shard_map/psum | solution.py:24
  83.7 0.8 copy-start.4
  83.7 0.8 copy-start.1
  83.7 305.9 %all-gather.7.cloned.1.call-start = ((), (), s32[]{:S(2)}) async-start(), calls=%async_computation.1 | async-start | bytes 5849088 | tf_op jit(solution)/shard_map/all_gather | solution.py:114
  84.4 372.4 %all-gather.9.cloned.1.call-start = ((), (), s32[]{:S(2)}) async-start(), calls=%async_computation.2 | async-start | bytes 3899392 | tf_op jit(solution)/shard_map/all_gather | solution.py:110
  85.2 1.5 copy-start.3
  85.2 3.4 copy-start.5
  85.2 5.3 copy-start.6
  312.7 1.6 copy-start.2
  463.2 15.3 %copy-start.7 = (bf16[224]{0:T(256)(128)(2,1)S(1)}, bf16[224]{0:T(256)(128)(2,1)}, u32[]{:S(2)}) copy-start(bf16[224]{0:T(256)(128)(2,1)} %param.22) | copy-start | bytes 1348
  464.4 97.1 %all-to-all-start = ((bf16[160,32,128]{2,0,1:T(8,128)(2,1)}), bf16[160,32,128]{2,0,1:T(8,128)(2,1)S(1)}, u32[]{:S(2)}, u32[]{:S(2)}) async-start(bf16[160,32,128]{2,0,1:T(8,128)(2,1)} %tile.9), calls=%async_computation | async-start | bytes 2621440 | tf_op jit(solution)/shard_map/all_to_all | solution.py:18
  477.9 85.0 %all-gather.11.cloned.1.call-start = ((), (), s32[]{:S(2)}) async-start(), calls=%async_computation.3 | async-start | bytes 1949696 | tf_op jit(solution)/shard_map/all_gather | solution.py:145
Sparse Core Ops, SparseCore 0:
  10.4 61.9 all-gather.12
  83.8 228.8 all-reduce.5
  315.8 73.7 all-gather.6
  392.5 64.3 all-gather.8
  481.4 58.0 all-gather.10
